TPU v7x, 256 devices: a whole 4x4x8 slice. The times are simulated.
256 devices in a mesh: seq: 64 (over y, z, core), head: 4 (over x).
Axes of the slice: x: 4, y: 4, z: 8, core: 2. Of those that a mesh axis runs over, the one named last changes fastest.
Arguments:
- queries: bfloat16 [8192, 1024], P('seq', 'head'), may hold values from -6 to 6
- raw_keys: bfloat16 [8192, 1024], P('seq', 'head'), may hold values from -6 to 6
- values: bfloat16 [8192, 1024], P('seq', 'head'), may hold values from -6 to 6
- write_rate: float32 [8192, 8], P('seq', 'head'), may hold values from 0.0005 to 1
- out_weight: bfloat16 [1024, 1024], P('head'), may hold values from -0.1875 to 0.1875
- out_grad: bfloat16 [8192, 1024], P('seq', 'head'), may hold values from -6 to 6
Outputs:
- layer_out: bfloat16 [8192, 1024], P('seq', 'head')
- query_grad: bfloat16 [8192, 1024], P('seq', 'head')
- key_grad: bfloat16 [8192, 1024], P('seq', 'head')
- value_grad: bfloat16 [8192, 1024], P('seq', 'head')
- rate_grad: float32 [8192, 8], P('seq', 'head')
All inputs are finite; a program needn't handle non-finite values.
Results may differ from a plain program's by a relative error of at most 0.0049.
Values may be sent and summed in bfloat16 or wider, within the bound.
No kernel may reach another device: no remote copies, remote signals or barrier semaphores. Data moves between devices by JAX's collectives and lax.ppermute only.
A program may use at most 128 MiB of HBM per device.

v0:
```python
import jax
import jax.numpy as jnp
from jax import lax
from jax.sharding import PartitionSpec as P

BLOCK = 64
epsilon = 1e-06
highest = lax.Precision.HIGHEST


def prefix(part, axis, combine, identity, reverse):
    count = lax.axis_size(axis)
    place = lax.axis_index(axis)
    ahead = count - 1 - place if reverse else place
    gathered = jax.tree.map(lambda a: lax.all_gather(a, axis), part)
    state = jax.tree.map(lambda a, e: jnp.zeros_like(a) + jnp.asarray(e, a.dtype), part, identity)

    def one(turn, state):
        source = count - 1 - turn if reverse else turn
        return combine(
            state, jax.tree.map(lambda a: lax.dynamic_index_in_dim(a, source, 0, False), gathered)
        )

    return lax.fori_loop(0, ahead, one, state)


def unit_rows(array):
    return array * lax.rsqrt(jnp.sum(array * array, -1, keepdims=True) + epsilon)


def to_blocks(array, head_count):
    rows = array.shape[0]
    head_width = array.shape[1] // head_count
    return array.reshape(rows // BLOCK, BLOCK, head_count, head_width).transpose(2, 0, 1, 3)


def rate_blocks(decay_rate):
    rows = decay_rate.shape[0]
    head_count = decay_rate.shape[1]
    return decay_rate.reshape(rows // BLOCK, BLOCK, head_count).transpose(2, 0, 1)


def from_blocks(block_outputs):
    block_count, head_count, size, head_width = block_outputs.shape
    return block_outputs.transpose(0, 2, 1, 3).reshape(block_count * size, head_count * head_width)


def block_factors(query_blocks, key_blocks, value_blocks, rate_parts):
    unit_query = unit_rows(query_blocks)
    unit_key = unit_rows(key_blocks)
    size = unit_key.shape[-2]
    identity_block = jnp.eye(size, dtype=jnp.float32)
    key_gram = jnp.einsum(
        "hncd,hnsd->hncs", unit_key * rate_parts[..., None], unit_key, precision=highest
    )
    strict_lower = jnp.tril(key_gram, -1)
    result = identity_block - strict_lower
    power_term = strict_lower
    span_done = 2
    while span_done < size:
        power_term = jnp.einsum("hnij,hnjk->hnik", power_term, power_term, precision=highest)
        result = result + jnp.einsum("hnij,hnjk->hnik", result, power_term, precision=highest)
        span_done = span_done * 2
    scaled = result * rate_parts[..., None, :]
    key_mix = jnp.einsum("hncs,hnsd->hncd", scaled, unit_key, precision=highest)
    value_mix = jnp.einsum("hncs,hnsd->hncd", scaled, value_blocks, precision=highest)
    causal_scores = jnp.tril(jnp.einsum("hncd,hnsd->hncs", unit_query, unit_key, precision=highest))
    return (unit_query, unit_key, key_mix, value_mix, causal_scores)


def run_blocks(factors, start_state):
    moved = tuple((jnp.moveaxis(member, 1, 0) for member in factors))

    def advance_block(state, pieces):
        unit_query, unit_key, key_mix, value_mix, causal_scores = pieces
        innovation = value_mix - jnp.einsum("hcd,hde->hce", key_mix, state, precision=highest)
        block_out = jnp.einsum("hcd,hde->hce", unit_query, state, precision=highest)
        block_out = block_out + jnp.einsum(
            "hcs,hse->hce", causal_scores, innovation, precision=highest
        )
        state = state + jnp.einsum("hcd,hce->hde", unit_key, innovation, precision=highest)
        return (state, block_out)

    return lax.scan(advance_block, start_state, moved)


def compose(earlier, later):
    early_map, early_shift = earlier
    late_map, late_shift = later
    joined_map = jnp.einsum("hij,hjk->hik", late_map, early_map, precision=highest)
    joined_shift = jnp.einsum("hij,hjk->hik", late_map, early_shift, precision=highest) + late_shift
    return (joined_map, joined_shift)


def body(queries, raw_keys, values, write_rate, out_weight, out_grad):
    head_count = write_rate.shape[1]
    head_width = queries.shape[1] // head_count
    token_count = queries.shape[0]

    def factor_inputs(float_query, float_key, float_value, rates):
        return block_factors(
            to_blocks(float_query, head_count),
            to_blocks(float_key, head_count),
            to_blocks(float_value, head_count),
            rate_blocks(rates),
        )

    factors, pull_factors = jax.vjp(
        factor_inputs,
        queries.astype(jnp.float32),
        raw_keys.astype(jnp.float32),
        values.astype(jnp.float32),
        write_rate,
    )
    unit_query, unit_key, key_mix, value_mix, causal_scores = factors
    identity_heads = jnp.broadcast_to(
        jnp.eye(head_width, dtype=jnp.float32), (head_count, head_width, head_width)
    )
    zero_heads = jnp.zeros((head_count, head_width, head_width), jnp.float32)
    widened = (
        unit_query,
        unit_key,
        key_mix,
        jnp.concatenate([jnp.zeros_like(value_mix), value_mix], -1),
        causal_scores,
    )
    joined_state, joined_outputs = run_blocks(
        widened, jnp.concatenate([identity_heads, zero_heads], -1)
    )
    transition = joined_state[..., :head_width]
    offset = joined_state[..., head_width:]
    query_effect = joined_outputs[..., :head_width]
    attended_grad = lax.dot_general(
        lax.all_gather(out_grad, "head", axis=1, tiled=True),
        out_weight,
        (((1,), (1,)), ((), ())),
        preferred_element_type=jnp.float32,
    )
    grad_blocks = attended_grad.reshape(
        token_count // BLOCK, BLOCK, head_count, head_width
    ).transpose(0, 2, 1, 3)
    local_adjoint = jnp.einsum("nhcd,nhce->hde", query_effect, grad_blocks, precision=highest)
    unused_map, entry_state = prefix(
        (transition, offset), "seq", compose, (identity_heads, zero_heads), False
    )
    unused_adjoint_map, exit_adjoint = prefix(
        (jnp.swapaxes(transition, 1, 2), local_adjoint),
        "seq",
        compose,
        (identity_heads, zero_heads),
        True,
    )

    def run_from_entry(factor_tuple):
        return run_blocks(factor_tuple, entry_state)

    (final_state, block_outputs), pull_run = jax.vjp(run_from_entry, factors)
    factor_grads = pull_run((exit_adjoint, grad_blocks))
    query_part, key_part, value_part, rate_grad = pull_factors(factor_grads[0])
    attended_bf = from_blocks(block_outputs).astype(jnp.bfloat16)
    partial_out = jnp.dot(attended_bf, out_weight, preferred_element_type=jnp.float32)
    layer_out = lax.psum_scatter(partial_out, "head", scatter_dimension=1, tiled=True).astype(
        jnp.bfloat16
    )
    return (
        layer_out,
        query_part.astype(jnp.bfloat16),
        key_part.astype(jnp.bfloat16),
        value_part.astype(jnp.bfloat16),
        rate_grad,
    )


def solution(mesh):
    placed = (
        P("seq", "head"),
        P("seq", "head"),
        P("seq", "head"),
        P("seq", "head"),
        P("head", None),
        P("seq", "head"),
    )
    return jax.shard_map(
        body,
        mesh=mesh,
        in_specs=placed,
        out_specs=(
            P("seq", "head"),
            P("seq", "head"),
            P("seq", "head"),
            P("seq", "head"),
            P("seq", "head"),
        ),
        check_vma=False,
    )
```

profile of v0, /device:TPU:8, one launch (start us, length us, event | category | flops | bytes accessed | tf_op | source)
XLA Modules:
  0.0 506.4 jit_solution(13383869806528043871)
XLA Ops:
  16.5 4.0 while.78
  20.5 12.6 %all_gather.33 = bf16[128,1024]{1,0:T(8,128)(2,1)S(1)} all-gather(bf16[128,256]{1,0:T(8,128)(2,1)S(1)} %copy-done.15), channel_id=1, replica_groups=mesh['seq'=64,'head'=4] {'head'}, dimensions={1}, use_global_device_ids=true | all-gather | bytes 327680 | tf_op jit(solution)/shard_map/all_gather | solution.py:134
  33.5 1.9 convolution_bitcast_fusion.4
  39.1 80.6 %all-gather.15.cloned.1.call-done = f32[128,128,128]{2,1,0:T(8,128)} async-done(((f32[2,128,128]{2,1,0:T(8,128)}), f32[128,128,128]{2,1,0:T(8,128)}) %all-gather.15.cloned.1.call-update) | async-done | bytes 8388624 | tf_op jit(solution)/shard_map/all_gather | solution.py:15
  119.6 82.6 %all-gather.13.cloned.1.call-done = f32[128,128,128]{2,1,0:T(8,128)} async-done(((f32[2,128,128]{2,1,0:T(8,128)}), f32[128,128,128]{2,1,0:T(8,128)}) %all-gather.13.cloned.1.call-update) | async-done | bytes 8388624 | tf_op jit(solution)/shard_map/all_gather | solution.py:15
  202.2 60.8 %while.81 = (s32[]{:T(128)}, f32[2,128,128]{2,1,0:T(8,128)S(1)}, s32[]{:T(128)}, f32[64,2,128,128]{3,2,1,0:T(8,128)}, f32[64,2,128,128]{3,2,1,0:T(8,128)}, /*index=5*/s32[]{:T(128)}, s32[]{:T(128)}, s32[]{:T(128)}, s32[]{:T(128)}) while((s32[]{:T(128)}, f32[2,128,128]{2,1,0:T(8,128)S(1)}, s32[]{:T(128)}, f32[64,2,128,128]{3,2,1,0:T(8,128)}, ...), condition=%wide.region_10.11_spmd, body=%wide.region_9.10_spmd.sunk | while | flops 50364420 | bytes 787595 | solution.py:24
  213.9 1.2 convolution_add_fusion.38
  215.2 1.3 convolution_add_fusion.38
  219.1 1.2 convolution_add_fusion.38
  221.7 1.2 convolution_add_fusion.38
  225.6 1.2 convolution_add_fusion.38
  228.1 1.2 convolution_add_fusion.38
  229.4 1.2 convolution_add_fusion.38
  241.1 1.2 convolution_add_fusion.38
  252.7 1.2 convolution_add_fusion.38
  257.9 1.3 convolution_add_fusion.38
  259.2 1.3 convolution_add_fusion.38
  263.1 21.8 %all-gather.9.cloned.1.call-done = f32[128,128,128]{2,1,0:T(8,128)} async-done(((f32[2,128,128]{2,1,0:T(8,128)}), f32[128,128,128]{2,1,0:T(8,128)}) %all-gather.9.cloned.1.call-update) | async-done | bytes 8388624 | tf_op jit(solution)/shard_map/all_gather | solution.py:15
  284.9 82.4 %all-gather.11.cloned.1.call-done = f32[128,128,128]{2,1,0:T(8,128)} async-done(((f32[2,128,128]{2,1,0:T(8,128)}), f32[128,128,128]{2,1,0:T(8,128)}) %all-gather.11.cloned.1.call-update) | async-done | bytes 8388624 | tf_op jit(solution)/shard_map/all_gather | solution.py:15
  367.3 20.8 %while.79 = (s32[]{:T(128)}, f32[2,128,128]{2,1,0:T(8,128)S(1)}, s32[]{:T(128)}, f32[64,2,128,128]{3,2,1,0:T(8,128)}, f32[64,2,128,128]{3,2,1,0:T(8,128)}, /*index=5*/s32[]{:T(128)}, s32[]{:T(128)}, s32[]{:T(128)}) while((s32[]{:T(128)}, f32[2,128,128]{2,1,0:T(8,128)S(1)}, s32[]{:T(128)}, f32[64,2,128,128]{3,2,1,0:T(8,128)}, ...), condition=%wide.region_5.6_spmd, body=%wide.region_4.5_spmd.sunk | while | flops 50364420 | bytes 787575 | solution.py:24
  388.2 3.5 while.80
  394.3 10.4 %while.82 = (s32[]{:T(128)}, f32[2,128,128]{2,1,0:T(8,128)S(1)}, f32[2,2,64,128]{3,2,0,1:T(8,128)}, f32[2,2,64,128]{3,2,0,1:T(8,128)}, f32[2,2,64,128]{3,2,1,0:T...) while((s32[]{:T(128)}, f32[2,128,128]{2,1,0:T(8,128)S(1)}, ...), condition=%wide.region_12.13_spmd, body=%wide.region_11.12_spmd.sunk | while | flops 176275456 | bytes 2367137 | solution.py:84
  420.9 77.4 %reduce-scatter.2.cloned.1.call-done = f32[128,256]{1,0:T(8,128)} async-done(((f32[128,1024]{1,0:T(8,128)}), f32[128,256]{1,0:T(8,128)}) %reduce-scatter.2.cloned.1.call-update) | async-done | bytes 131088 | tf_op jit(solution)/shard_map/reduce_scatter | solution.py:162
  498.3 1.5 convert_element_type.51
  (298 shorter events, 114.2 us)
Async XLA Ops:
  7.2 25.9 %copy-start = (bf16[256,1024]{1,0:T(8,128)(2,1)S(1)}, bf16[256,1024]{1,0:T(8,128)(2,1)}, u32[]{:S(2)}) copy-start(bf16[256,1024]{1,0:T(8,128)(2,1)} %param.20) | copy-start | bytes 1572868
  7.2 112.4 %all-gather.15.cloned.1.call-start = ((), (), s32[]{:S(2)}) async-start(), calls=%async_computation.5 | async-start | bytes 8519680 | tf_op jit(solution)/shard_map/all_gather | solution.py:15
  7.2 4.0 copy-start.10
  8.4 3.7 copy-start.20
  9.4 2.7 copy-start.18
  10.3 4.7 copy-start.16
  12.4 8.1 %copy-start.15 = (bf16[128,256]{1,0:T(8,128)(2,1)S(1)}, bf16[128,256]{1,0:T(8,128)(2,1)}, u32[]{:S(2)}) copy-start(bf16[128,256]{1,0:T(8,128)(2,1)} %param.21) | copy-start | bytes 196612
  12.7 3.8 copy-start.1
  35.4 166.8 %all-gather.13.cloned.1.call-start = ((), (), s32[]{:S(2)}) async-start(), calls=%async_computation.4 | async-start | bytes 8519680 | tf_op jit(solution)/shard_map/all_gather | solution.py:15
  37.0 247.8 %all-gather.9.cloned.1.call-start = ((), (), s32[]{:S(2)}) async-start(), calls=%async_computation.2 | async-start | bytes 8519680 | tf_op jit(solution)/shard_map/all_gather | solution.py:15
  37.8 329.5 %all-gather.11.cloned.1.call-start = ((), (), s32[]{:S(2)}) async-start(), calls=%async_computation.3 | async-start | bytes 8519680 | tf_op jit(solution)/shard_map/all_gather | solution.py:15
  38.3 460.0 %reduce-scatter.2.cloned.1.call-start = ((), (), s32[]{:S(2)}) async-start(), calls=%async_computation.1 | async-start | bytes 655360 | tf_op jit(solution)/shard_map/reduce_scatter | solution.py:162
  392.4 17.0 %copy-start.2 = (f32[2,2,64,64]{3,2,1,0:T(8,128)S(1)}, f32[2,2,64,64]{3,2,1,0:T(8,128)}, u32[]{:S(2)}) copy-start(f32[2,2,64,64]{3,2,1,0:T(8,128)} %copy-done.1) | copy-start | bytes 196612
  394.3 17.3 %copy-start.4 = (f32[2,2,64,64]{3,2,1,0:T(8,128)S(1)}, f32[2,2,64,64]{3,2,1,0:T(8,128)}, u32[]{:S(2)}) copy-start(f32[2,2,64,64]{3,2,1,0:T(8,128)} %copy-done.3) | copy-start | bytes 196612
  404.7 8.1 %copy-start.11 = (f32[64,64]{1,0:T(8,128)S(1)}, f32[64,64]{1,0:T(8,128)}, u32[]{:S(2)}) copy-start(f32[64,64]{1,0:T(8,128)} %copy-done.10) | copy-start | bytes 49156
  404.7 9.2 %copy-start.14 = (pred[64,64]{1,0:T(8,128)(4,1)S(1)}, pred[64,64]{1,0:T(8,128)(4,1)}, u32[]{:S(2)}) copy-start(pred[64,64]{1,0:T(8,128)(4,1)} %copy-done.13) | copy-start | bytes 12292
  404.7 10.0 %copy-start.7 = (f32[2,2,64,64]{3,2,1,0:T(8,128)S(1)}, f32[2,2,64,64]{3,2,1,0:T(8,128)}, u32[]{:S(2)}) copy-start(f32[2,2,64,64]{3,2,1,0:T(8,128)} %get-tuple-element.516) | copy-start | bytes 196612
  404.7 10.0 %copy-start.17 = (f32[2,2,64]{2,1,0:T(2,128)S(1)}, f32[2,2,64]{2,1,0:T(2,128)}, u32[]{:S(2)}) copy-start(f32[2,2,64]{2,1,0:T(2,128)} %copy-done.16) | copy-start | bytes 3076
  404.7 10.5 %copy-start.6 = (f32[2,2,64,128]{3,2,0,1:T(8,128)S(1)}, f32[2,2,64,128]{3,2,0,1:T(8,128)}, u32[]{:S(2)}) copy-start(f32[2,2,64,128]{3,2,0,1:T(8,128)} %get-tuple-element.517) | copy-start | bytes 393220
  404.8 11.0 %copy-start.21 = (f32[2,2,64]{2,1,0:T(2,128)S(1)}, f32[2,2,64]{2,1,0:T(2,128)}, u32[]{:S(2)}) copy-start(f32[2,2,64]{2,1,0:T(2,128)} %copy-done.20) | copy-start | bytes 3076
  404.8 11.0 %copy-start.12 = (bf16[2,2,64,128]{3,2,1,0:T(8,128)(2,1)S(1)}, bf16[2,2,64,128]{3,2,1,0:T(8,128)(2,1)}, u32[]{:S(2)}) copy-start(bf16[2,2,64,128]{3,2,1,0:T(8,128)(2,1)} %get-tuple-element.510) | copy-start | bytes 196612
  404.8 13.7 %copy-start.8 = (f32[2,2,64,128]{3,2,1,0:T(8,128)S(1)}, f32[2,2,64,128]{3,2,1,0:T(8,128)}, u32[]{:S(2)}) copy-start(f32[2,2,64,128]{3,2,1,0:T(8,128)} %get-tuple-element.519) | copy-start | bytes 393220
  404.8 14.8 %copy-start.5 = (f32[2,2,64,128]{3,2,0,1:T(8,128)S(1)}, f32[2,2,64,128]{3,2,0,1:T(8,128)}, u32[]{:S(2)}) copy-start(f32[2,2,64,128]{3,2,0,1:T(8,128)} %get-tuple-element.515) | copy-start | bytes 393220
  404.8 15.3 %copy-start.19 = (f32[2,2,64]{2,1,0:T(2,128)S(1)}, f32[2,2,64]{2,1,0:T(2,128)}, u32[]{:S(2)}) copy-start(f32[2,2,64]{2,1,0:T(2,128)} %copy-done.18) | copy-start | bytes 3076
  (3 other events, 2.8 us)
Sparse Core Ops, SparseCore 0:
  35.6 84.0 all-gather.14
  122.4 79.7 all-gather.12
  205.0 79.8 all-gather.8
  287.5 79.7 all-gather.10
  417.1 81.1 reduce-scatter.1
where the time goes:
time: 508 us; the launch traced here: 506 us
  waiting for transfers between devices  346 us (68%)
  matrix products  115 us (23%)
  between operations  14.6 us (3%)
  blocking collectives  12.6 us (2%)
  local copies, waits for them, and re-layouts  12 us (2%)
    all_gather x4, waiting for transfers between devices, prefix(): gathered = jax.tree.map(lambda a: lax.all_gather(a, axis), part)  267 us
    dot_general x63, matrix products, compose(): jnp.einsum('hij,hjk->hik', late_map, early_shift, precision=highest)  78.3 us
    reduce_scatter x1, waiting for transfers between devices, body(): lax.psum_scatter(partial_out, 'head', scatter_dimension=1, tiled=True)  77.4 us
    all_gather x1, blocking collectives, body(): lax.all_gather(out_grad, 'head', axis=1, tiled=True)  12.6 us
  transfers between devices with their start and end apart: 5, of which 5 were waited for; matrix products, arithmetic and copies ran while one was open for 13% of the time, Pallas kernels for 0%

commit v1 on v0

--- a/solution.py
+++ b/solution.py
@@ -130,8 +130,35 @@
     transition = joined_state[..., :head_width]
     offset = joined_state[..., head_width:]
     query_effect = joined_outputs[..., :head_width]
+
+    def _see_leaf(row_data, peer_axis):
+        out_arr = lax.axis_size(peer_axis)
+        oldest = lax.axis_index(peer_axis)
+        block_last, part_next, built = (out_arr, oldest, row_data.shape[1])
+        windows = tuple(((i0, (i0 + 1) % block_last) for i0 in range(block_last)))
+        v1 = jnp.zeros(
+            (*row_data.shape[:1], block_last * built, *row_data.shape[2:]), row_data.dtype
+        )
+        v1 = lax.dynamic_update_slice_in_dim(v1, row_data, part_next * built, axis=1)
+        all_blocks = tuple(((i0, (i0 - 1) % block_last) for i0 in range(block_last)))
+        ready = aux = row_data
+        tick = 1
+        mat_out = block_last // 2
+        while tick < mat_out + 1:
+            ready = lax.ppermute(ready, axis_name=peer_axis, perm=windows)
+            v1 = lax.dynamic_update_slice_in_dim(
+                v1, ready, (part_next - tick) % block_last * built, axis=1
+            )
+            if tick < block_last - mat_out:
+                aux = lax.ppermute(aux, perm=all_blocks, axis_name=peer_axis)
+                v1 = lax.dynamic_update_slice_in_dim(
+                    v1, aux, (part_next + tick) % block_last * built, axis=1
+                )
+            tick += 1
+        return v1
+
     attended_grad = lax.dot_general(
-        lax.all_gather(out_grad, "head", axis=1, tiled=True),
+        _see_leaf(out_grad, "head"),
         out_weight,
         (((1,), (1,)), ((), ())),
         preferred_element_type=jnp.float32,

time: 508 us -> 475 us (0.935)
  the two profiles are of different devices: /device:TPU:8 before, /device:TPU:2 now
where the time goes in v1:
time: 475 us; the launch traced here: 473 us
  waiting for transfers between devices  321 us (68%)
  matrix products  115 us (24%)
  between operations  14.6 us (3%)
  local copies, waits for them, and re-layouts  13.3 us (3%)
    all_gather x4, waiting for transfers between devices, prefix(): gathered = jax.tree.map(lambda a: lax.all_gather(a, axis), part)  313 us
    dot_general x63, matrix products, compose(): jnp.einsum('hij,hjk->hik', late_map, early_shift, precision=highest)  78.2 us
  transfers between devices with their start and end apart: 8, of which 6 were waited for; matrix products, arithmetic and copies ran while one was open for 24% of the time, Pallas kernels for 0%

profile of v1, /device:TPU:2, one launch (start us, length us, event | category | flops | bytes accessed | tf_op | source)
XLA Modules:
  0.0 473.1 jit_solution(11798860399108995909)
XLA Ops:
  16.8 4.0 while.78
  23.2 1.6 collective-permute-start
  25.7 2.1 collective-permute-done
  27.8 1.3 collective-permute-start.2
  29.1 4.1 collective-permute-done.2
  33.6 2.0 convolution_bitcast_fusion.4
  36.3 71.3 %all-gather.9.cloned.1.call-done = f32[128,128,128]{2,1,0:T(8,128)} async-done(((f32[2,128,128]{2,1,0:T(8,128)}), f32[128,128,128]{2,1,0:T(8,128)}) %all-gather.9.cloned.1.call-update) | async-done | bytes 8388624 | tf_op jit(solution)/shard_map/all_gather | solution.py:15
  107.7 82.6 %all-gather.11.cloned.1.call-done = f32[128,128,128]{2,1,0:T(8,128)} async-done(((f32[2,128,128]{2,1,0:T(8,128)}), f32[128,128,128]{2,1,0:T(8,128)}) %all-gather.11.cloned.1.call-update) | async-done | bytes 8388624 | tf_op jit(solution)/shard_map/all_gather | solution.py:15
  190.3 3.5 while.80
  195.8 77.1 %all-gather.13.cloned.1.call-done = f32[128,128,128]{2,1,0:T(8,128)} async-done(((f32[2,128,128]{2,1,0:T(8,128)}), f32[128,128,128]{2,1,0:T(8,128)}) %all-gather.13.cloned.1.call-update) | async-done | bytes 8388624 | tf_op jit(solution)/shard_map/all_gather | solution.py:15
  272.9 82.5 %all-gather.15.cloned.1.call-done = f32[128,128,128]{2,1,0:T(8,128)} async-done(((f32[2,128,128]{2,1,0:T(8,128)}), f32[128,128,128]{2,1,0:T(8,128)}) %all-gather.15.cloned.1.call-update) | async-done | bytes 8388624 | tf_op jit(solution)/shard_map/all_gather | solution.py:15
  355.4 81.6 %while.81 = (s32[]{:T(128)}, f32[2,128,128]{2,1,0:T(8,128)S(1)}, s32[]{:T(128)}, f32[64,2,128,128]{3,2,1,0:T(8,128)}, f32[64,2,128,128]{3,2,1,0:T(8,128)}, /*index=5*/s32[]{:T(128)}, s32[]{:T(128)}, s32[]{:T(128)}, s32[]{:T(128)}) while((s32[]{:T(128)}, f32[2,128,128]{2,1,0:T(8,128)S(1)}, s32[]{:T(128)}, f32[64,2,128,128]{3,2,1,0:T(8,128)}, ...), condition=%wide.region_10.11_spmd, body=%wide.region_9.10_spmd.sunk | while | flops 50364420 | bytes 787595 | solution.py:24
  356.7 1.2 convolution_add_fusion.38
  358.0 1.2 convolution_add_fusion.38
  365.8 1.2 convolution_add_fusion.38
  367.1 1.2 convolution_add_fusion.38
  369.7 1.2 convolution_add_fusion.38
  373.5 1.2 convolution_add_fusion.38
  376.1 1.2 convolution_add_fusion.38
  377.4 1.2 convolution_add_fusion.38
  381.3 1.2 convolution_add_fusion.38
  396.8 1.2 convolution_add_fusion.38
  439.6 10.4 %while.82 = (s32[]{:T(128)}, f32[2,128,128]{2,1,0:T(8,128)S(1)}, f32[2,2,64,128]{3,2,0,1:T(8,128)}, f32[2,2,64,128]{3,2,0,1:T(8,128)}, f32[2,2,64,128]{3,2,1,0:T...) while((s32[]{:T(128)}, f32[2,128,128]{2,1,0:T(8,128)S(1)}, ...), condition=%wide.region_12.13_spmd, body=%wide.region_11.12_spmd.sunk | while | flops 176275456 | bytes 2367137 | solution.py:84
  465.0 1.5 convert_element_type.51
  (302 shorter events, 117.0 us)
Async XLA Ops:
  7.2 26.1 %copy-start = (bf16[256,1024]{1,0:T(8,128)(2,1)S(1)}, bf16[256,1024]{1,0:T(8,128)(2,1)}, u32[]{:S(2)}) copy-start(bf16[256,1024]{1,0:T(8,128)(2,1)} %param.20) | copy-start | bytes 1572868
  7.2 100.5 %all-gather.9.cloned.1.call-start = ((), (), s32[]{:S(2)}) async-start(), calls=%async_computation.2 | async-start | bytes 8519680 | tf_op jit(solution)/shard_map/all_gather | solution.py:15
  7.2 4.0 copy-start.8
  8.4 6.9 %copy-start.17 = (f32[2,2,64]{2,1,0:T(2,128)}, f32[2,2,64]{2,1,0:T(2,128)S(1)}, u32[]{:S(2)}) copy-start(f32[2,2,64]{2,1,0:T(2,128)S(1)} %fusion.98) | copy-start | bytes 3076
  9.4 5.9 %copy-start.15 = (f32[2,2,64]{2,1,0:T(2,128)}, f32[2,2,64]{2,1,0:T(2,128)S(1)}, u32[]{:S(2)}) copy-start(f32[2,2,64]{2,1,0:T(2,128)S(1)} %fusion.97) | copy-start | bytes 3076
  10.3 5.0 %copy-start.13 = (f32[2,2,64]{2,1,0:T(2,128)}, f32[2,2,64]{2,1,0:T(2,128)S(1)}, u32[]{:S(2)}) copy-start(f32[2,2,64]{2,1,0:T(2,128)S(1)} %get-tuple-element.713) | copy-start | bytes 3076
  13.8 9.4 %copy-start.12 = (bf16[128,256]{1,0:T(8,128)(2,1)S(1)}, bf16[128,256]{1,0:T(8,128)(2,1)}, u32[]{:S(2)}) copy-start(bf16[128,256]{1,0:T(8,128)(2,1)} %param.21) | copy-start | bytes 196612
  21.6 168.7 %all-gather.11.cloned.1.call-start = ((), (), s32[]{:S(2)}) async-start(), calls=%async_computation.3 | async-start | bytes 8519680 | tf_op jit(solution)/shard_map/all_gather | solution.py:15
  22.3 250.6 %all-gather.13.cloned.1.call-start = ((), (), s32[]{:S(2)}) async-start(), calls=%async_computation.4 | async-start | bytes 8519680 | tf_op jit(solution)/shard_map/all_gather | solution.py:15
  23.1 332.2 %all-gather.15.cloned.1.call-start = ((), (), s32[]{:S(2)}) async-start(), calls=%async_computation.5 | async-start | bytes 8519680 | tf_op jit(solution)/shard_map/all_gather | solution.py:15
  23.2 4.6 collective-permute-start
  24.8 4.3 collective-permute-start.1
  27.8 5.5 %collective-permute-start.2 = (bf16[128,256]{1,0:T(8,128)(2,1)S(1)}, bf16[128,256]{1,0:T(8,128)(2,1)S(1)}, u32[]{:S(2)}, u32[]{:S(2)}) collective-permute-start(bf16[128,256]{1,0:T(8,128)(2,1)S(1)} %collective-permute-done), channel_id=1, source_target_pairs={{0,1},{1,2},{2,3},{3,0},{4,5},{5,6},{6,7},{7,4},{8,9},{9,10},{10,1... | collective-permute-start | bytes 196616 | tf_op jit(solution)/shard_map/ppermute | solution.py:148
  35.6 429.4 %reduce-scatter.2.cloned.1.call-start = ((), (), s32[]{:S(2)}) async-start(), calls=%async_computation.1 | async-start | bytes 655360 | tf_op jit(solution)/shard_map/reduce_scatter | solution.py:189
  439.6 17.3 %copy-start.2 = (f32[2,2,64,64]{3,2,1,0:T(8,128)S(1)}, f32[2,2,64,64]{3,2,1,0:T(8,128)}, u32[]{:S(2)}) copy-start(f32[2,2,64,64]{3,2,1,0:T(8,128)} %copy-done.1) | copy-start | bytes 196612
  450.0 8.0 %copy-start.9 = (f32[64,64]{1,0:T(8,128)S(1)}, f32[64,64]{1,0:T(8,128)}, u32[]{:S(2)}) copy-start(f32[64,64]{1,0:T(8,128)} %copy-done.8) | copy-start | bytes 49156
  450.0 9.2 %copy-start.11 = (pred[64,64]{1,0:T(8,128)(4,1)S(1)}, pred[64,64]{1,0:T(8,128)(4,1)}, u32[]{:S(2)}) copy-start(pred[64,64]{1,0:T(8,128)(4,1)} %copy-done.10) | copy-start | bytes 12292
  450.0 10.0 %copy-start.5 = (f32[2,2,64,64]{3,2,1,0:T(8,128)S(1)}, f32[2,2,64,64]{3,2,1,0:T(8,128)}, u32[]{:S(2)}) copy-start(f32[2,2,64,64]{3,2,1,0:T(8,128)} %get-tuple-element.516) | copy-start | bytes 196612
  450.0 10.0 %copy-start.14 = (f32[2,2,64]{2,1,0:T(2,128)S(1)}, f32[2,2,64]{2,1,0:T(2,128)}, u32[]{:S(2)}) copy-start(f32[2,2,64]{2,1,0:T(2,128)} %copy-done.13) | copy-start | bytes 3076
  450.0 10.5 %copy-start.4 = (f32[2,2,64,128]{3,2,0,1:T(8,128)S(1)}, f32[2,2,64,128]{3,2,0,1:T(8,128)}, u32[]{:S(2)}) copy-start(f32[2,2,64,128]{3,2,0,1:T(8,128)} %get-tuple-element.517) | copy-start | bytes 393220
  450.0 11.0 %copy-start.18 = (f32[2,2,64]{2,1,0:T(2,128)S(1)}, f32[2,2,64]{2,1,0:T(2,128)}, u32[]{:S(2)}) copy-start(f32[2,2,64]{2,1,0:T(2,128)} %copy-done.17) | copy-start | bytes 3076
  450.1 12.5 %copy-start.6 = (f32[2,2,64,128]{3,2,1,0:T(8,128)S(1)}, f32[2,2,64,128]{3,2,1,0:T(8,128)}, u32[]{:S(2)}) copy-start(f32[2,2,64,128]{3,2,1,0:T(8,128)} %get-tuple-element.519) | copy-start | bytes 393220
  450.1 13.6 %copy-start.3 = (f32[2,2,64,128]{3,2,0,1:T(8,128)S(1)}, f32[2,2,64,128]{3,2,0,1:T(8,128)}, u32[]{:S(2)}) copy-start(f32[2,2,64,128]{3,2,0,1:T(8,128)} %get-tuple-element.515) | copy-start | bytes 393220
  450.1 14.1 %copy-start.16 = (f32[2,2,64]{2,1,0:T(2,128)S(1)}, f32[2,2,64]{2,1,0:T(2,128)}, u32[]{:S(2)}) copy-start(f32[2,2,64]{2,1,0:T(2,128)} %copy-done.15) | copy-start | bytes 3076
  (3 other events, 2.0 us)
Sparse Core Ops, SparseCore 0:
  21.7 85.9 all-gather.8
  110.4 79.7 all-gather.10
  193.0 79.8 all-gather.12
  275.6 79.7 all-gather.14
  357.8 18.8 reduce-scatter.1
